TPU v7x, 256 devices: a whole 4x4x8 slice. The times are simulated.
256 devices in a mesh: row: 4 (over y), col: 4 (over x), dp: 16 (over z, core).
Axes of the slice: x: 4, y: 4, z: 8, core: 2. Of those that a mesh axis runs over, the one named last changes fastest.
Arguments:
- hidden_states: bfloat16 [16384, 1536], P(('dp', 'row'), 'col'), may hold values from -18 to 18
- w_query: bfloat16 [1536, 1536], P('col', 'row'), may hold values from -0.102062073 to 0.102062073
- w_key_value: bfloat16 [1536, 512], P('col'), may hold values from -0.102062073 to 0.102062073
- adapter_down: bfloat16 [1024, 1536, 16], P('dp', 'col'), may hold values from -0.15625 to 0.15625
- adapter_up: bfloat16 [1024, 16, 1536], P('dp', None, 'row'), may hold values from -1.5 to 1.5
- req_lengths: int32 [16, 8], replicated, may hold values from 1 to 160, 960 in all within a row
- req_adapter: int32 [16, 8], replicated, may hold values from 0 to 1023, as said below
Outputs:
- attention: bfloat16 [16384, 1536], P(('dp', 'col'), 'row')
- kv_cache: bfloat16 [16384, 512], P(('dp', 'col'))
Inputs may be any that keep to these rules, and one draw needn't show every extreme that they name: `req_lengths`: the lengths of one block sum to 960, and each block has a request of exactly 160 tokens. `req_adapter`: adapters k * 64 to (k + 1) * 64 - 1 are those of index k of dp; the requests of one block use adapters of one index of dp at most 1 times, and some index of dp is used exactly that often by every block.
All inputs are finite; a program needn't handle non-finite values.
Results may differ from a plain program's by a relative error of at most 0.0072.
Values may be sent and summed in bfloat16 or wider, within the bound.
No kernel may reach another device: no remote copies, remote signals or barrier semaphores. Data moves between devices by JAX's collectives and lax.ppermute only.
A program may use at most 128 MiB of HBM per device.

v0:
```python
import math
import jax
import jax.numpy as jnp
from jax import lax
from jax.sharding import PartitionSpec as P

HEAD_DIM = 128
MOST_LEN = 160
masked_score = -1e30


def block_layout(lengths_row, block_len):
    prefix_len = block_len - jnp.sum(lengths_row)
    ends_at = jnp.cumsum(lengths_row) + prefix_len
    starts = ends_at - lengths_row
    positions = jnp.arange(block_len, dtype=jnp.int32)
    segment = jnp.sum((positions[:, None] >= starts[None, :]).astype(jnp.int32), axis=1)
    return (starts, segment, positions)


def slot_numbers(holders):
    request_total = holders.shape[0]
    ordering = jnp.arange(request_total, dtype=jnp.int32)
    earlier = ordering[None, :] < ordering[:, None]
    same_holder = holders[:, None] == holders[None, :]
    return jnp.sum((earlier & same_holder).astype(jnp.int32), axis=1)


def make_attend(query_rows, segment, first_row, kv_group, head_size, kv_half):
    own_rows = query_rows.shape[0]
    heads_here = query_rows.shape[1] // head_size
    query_heads = query_rows.reshape(own_rows, heads_here, head_size)
    query_pos = first_row + jnp.arange(own_rows, dtype=jnp.int32)
    query_seg = lax.dynamic_slice_in_dim(segment, first_row, own_rows, 0)
    score_scale = 1.0 / math.sqrt(head_size)

    def attend(state_in, key_block, key_start):
        running_max, running_sum, running_out = state_in
        block_size = key_block.shape[0]
        key_rows = lax.dynamic_slice_in_dim(key_block, kv_group * head_size, head_size, 1)
        values = lax.dynamic_slice_in_dim(key_block, kv_half + kv_group * head_size, head_size, 1)
        key_pos = jnp.arange(block_size, dtype=jnp.int32)
        allowed = (key_pos[None, :] <= query_pos[:, None]) & (
            (segment[None, :] == query_seg[:, None]) | (segment[None, :] == 0)
        )
        scores = (
            jnp.einsum("qhd,kd->hqk", query_heads, key_rows, preferred_element_type=jnp.float32)
            * score_scale
        )
        scores = jnp.where(allowed[None], scores, masked_score)
        new_max = jnp.maximum(running_max, jnp.max(scores, axis=2))
        weights = jnp.where(allowed[None], jnp.exp(scores - new_max[:, :, None]), 0.0)
        running_sum = jnp.sum(weights, axis=2)
        running_out = jnp.einsum(
            "hqk,kd->hqd", weights.astype(jnp.bfloat16), values, preferred_element_type=jnp.float32
        )
        return (new_max, running_sum, running_out)

    initial = (
        jnp.full((heads_here, own_rows), masked_score, jnp.float32),
        jnp.zeros((heads_here, own_rows), jnp.float32),
        jnp.zeros((heads_here, own_rows, head_size), jnp.float32),
    )
    return (attend, initial)


def body(hidden_states, w_query, w_key_value, adapter_down, adapter_up, req_lengths, req_adapter):
    dp_size = lax.axis_size("dp")
    block_index = lax.axis_index("dp")
    col_index = lax.axis_index("col")
    row_index = lax.axis_index("row")
    gathered = lax.all_gather(hidden_states, "row", axis=0, tiled=True)
    block_len = gathered.shape[0]
    query_cols = w_query.shape[1]
    kv_cols = w_key_value.shape[1]
    kv_half = kv_cols // 2
    head_size = HEAD_DIM
    heads_here = query_cols // head_size
    heads_total = heads_here * lax.axis_size("row")
    kv_heads = kv_half // head_size
    kv_group = row_index * heads_here // (heads_total // kv_heads)
    own_rows = block_len // lax.axis_size("col")
    first_row = col_index * own_rows
    held_sets = adapter_down.shape[0]
    width_here = adapter_down.shape[1]
    rank_size = adapter_down.shape[2]
    lengths_row = req_lengths[block_index]
    adapters_row = req_adapter[block_index]
    requests = lengths_row.shape[0]
    starts, segment, positions = block_layout(lengths_row, block_len)
    request_of = jnp.clip(segment - 1, 0, requests - 1)
    in_request = segment > 0
    holders = adapters_row // held_sets
    slot_of = slot_numbers(holders)
    per_holder = (requests + dp_size - 1) // dp_size
    longest = MOST_LEN
    target_ids = jnp.arange(dp_size, dtype=jnp.int32)[:, None, None]
    slot_ids = jnp.arange(per_holder, dtype=jnp.int32)[None, :, None]
    pairing = (holders[None, None, :] == target_ids) & (slot_of[None, None, :] == slot_ids)
    pair_int = pairing.astype(jnp.int32)
    slot_start = jnp.sum(pair_int * starts[None, None, :], axis=2)
    slot_len = jnp.sum(pair_int * lengths_row[None, None, :], axis=2)
    slot_adapter = jnp.where(
        jnp.any(pairing, axis=2),
        jnp.sum(pair_int * (adapters_row % held_sets)[None, None, :], axis=2),
        -1,
    )
    offsets = jnp.arange(longest, dtype=jnp.int32)
    token_at = slot_start[:, :, None] + offsets[None, None, :]
    live_rows = offsets[None, None, :] < slot_len[:, :, None]
    outgoing = jnp.where(
        live_rows[..., None],
        gathered[jnp.clip(token_at, 0, block_len - 1)],
        jnp.zeros((), gathered.dtype),
    )
    flat_down = jnp.transpose(adapter_down, (1, 0, 2)).reshape(width_here, held_sets * rank_size)
    flat_up = adapter_up.reshape(held_sets * rank_size, query_cols).astype(jnp.float32)
    rank_owner = jnp.arange(held_sets * rank_size, dtype=jnp.int32) // rank_size
    sent_rows = lax.all_to_all(outgoing, "dp", split_axis=0, concat_axis=0, tiled=True)
    sent_ids = lax.all_to_all(
        slot_adapter.astype(jnp.bfloat16), "dp", split_axis=0, concat_axis=0, tiled=True
    )
    reduced = jnp.einsum("nkld,da->nkla", sent_rows, flat_down, preferred_element_type=jnp.float32)
    kept_cols = rank_owner[None, None, :] == sent_ids.astype(jnp.int32)[:, :, None]
    reduced = jnp.where(kept_cols[:, :, None, :], reduced, 0.0)
    adapter_part = jnp.einsum("nkla,af->nklf", reduced, flat_up, precision=lax.Precision.HIGHEST)
    returned = lax.all_to_all(adapter_part, "dp", split_axis=0, concat_axis=0, tiled=True)
    flat_index = (holders[request_of] * per_holder + slot_of[request_of]) * longest + jnp.clip(
        positions - starts[request_of], 0, longest - 1
    )
    adapter_term = returned.reshape(-1, query_cols)[flat_index]
    adapter_term = jnp.where(in_request[:, None], adapter_term, 0.0)
    both_weights = jnp.concatenate([w_query, w_key_value], axis=1)
    partial_value = jnp.dot(gathered, both_weights, preferred_element_type=jnp.float32)
    summed = lax.psum_scatter(
        partial_value
        + jnp.concatenate(
            [adapter_term, jnp.zeros((own_rows * lax.axis_size("col"), kv_cols), jnp.float32)],
            axis=1,
        ),
        "col",
        scatter_dimension=0,
        tiled=True,
    )
    query_rows = summed[:, :query_cols].astype(jnp.bfloat16)
    kv_cache = summed[:, query_cols:].astype(jnp.bfloat16)
    attend, initial = make_attend(query_rows, segment, first_row, kv_group, head_size, kv_half)
    running_max, running_sum, running_out = attend(
        initial, lax.all_gather(kv_cache, "col", axis=0, tiled=True), jnp.int32(0)
    )
    attention = (running_out / running_sum[:, :, None]).astype(jnp.bfloat16)
    attention = jnp.transpose(attention, (1, 0, 2)).reshape(own_rows, query_cols)
    return (attention, kv_cache)


def solution(mesh):
    return jax.shard_map(
        body,
        mesh=mesh,
        in_specs=(
            P(("dp", "row"), "col"),
            P("col", "row"),
            P("col", None),
            P("dp", "col", None),
            P("dp", None, "row"),
            P(),
            P(),
        ),
        out_specs=(P(("dp", "col"), "row"), P(("dp", "col"), None)),
        check_vma=False,
    )
```

profile of v0, /device:TPU:8, one launch (start us, length us, event | category | flops | bytes accessed | tf_op | source)
XLA Modules:
  0.0 303.4 jit_solution(6985747026854632109)
XLA Ops:
  7.2 1.5 fusion.34
  11.7 8.6 %all-to-all-start = ((bf16[16,1,1]{2,1,0:T(2,128)(2,1)}), bf16[16,1,1]{2,1,0:T(2,128)(2,1)}, u32[]{:S(2)}, u32[]{:S(2)}) async-start(bf16[16,1,1]{2,1,0:T(2,128)(2,1)} %copy.46), calls=%async_computation | async-start | bytes 16384 | tf_op jit(solution)/shard_map/all_to_all | solution.py:120
  20.5 14.9 %all_gather.6 = bf16[1024,384]{1,0:T(8,128)(2,1)S(1)} all-gather(bf16[256,384]{1,0:T(8,128)(2,1)} %param.7), channel_id=1, replica_groups=mesh['row'=4,'col'=4,'dp'=16] {'row'}, dimensions={0}, use_global_device_ids=true | all-gather | bytes 983040 | tf_op jit(solution)/shard_map/all_gather | solution.py:72
  35.5 7.5 %gather_fusion = bf16[2560,384]{1,0:T(8,128)(2,1)S(1)} fusion(bf16[1024,384]{1,0:T(8,128)(2,1)S(1)} %all_gather.6, s32[3072]{0:T(1024)S(1)} %pad_clamp_fusion), kind=kCustom, calls=%fused_computation | custom fusion | bytes 3942400 | tf_op jit(solution)/shard_map/gather | solution.py:113
  43.0 1.5 broadcast_select_fusion
  44.5 7.0 %all-to-all-start.1 = ((bf16[16,1,160,384]{3,2,1,0:T(8,128)(2,1)}), bf16[16,1,160,384]{3,2,1,0:T(8,128)(2,1)S(1)}, u32[]{:S(2)}, u32[]{:S(2)}) async-start(bf16[16,1,160,384]{3,2,1,0:T(8,128)(2,1)} %broadcast_select_fusion), calls=%async_computation.1 | async-start | bytes 3932160 | tf_op jit(solution)/shard_map/all_to_all | solution.py:119
  51.5 1.1 convert_reduce_fusion.1
  52.7 45.2 %all-to-all-done.1 = bf16[16,1,160,384]{3,2,1,0:T(8,128)(2,1)S(1)} async-done(((bf16[16,1,160,384]{3,2,1,0:T(8,128)(2,1)}), bf16[16,1,160,384]{3,2,1,0:T(8,128)(2,1)S(1)}, u32[]{:S(2)}, u32[]{:S(2)}) %all-to-all-start.1) | async-done | bytes 1966112 | tf_op jit(solution)/shard_map/all_to_all | solution.py:119
  97.9 3.0 fusion.10
  100.9 10.3 %fusion.7 = f32[16,1,160,384]{3,2,1,0:T(8,128)} fusion(bf16[1024,384,1]{1,0,2:T(8,128)(2,1)S(1)} %bitcast.109, f32[16,160,1024]{2,1,0:T(8,128)S(1)} %fusion.10, pred[16,1024]{1,0:T(8,128)(4,1)S(1)} %broadcast_compare_fusion), kind=kOutput, calls=%fused_computation.12 | convolution fusion | flops 12082216960 | bytes 15220736 | tf_op jit(solution)/shard_map/nkla,af->nklf/dot_general | solution.py:126
  111.2 4.8 %all-to-all-start.2 = ((f32[16,1,160,384]{3,2,1,0:T(8,128)}), f32[16,1,160,384]{3,2,1,0:T(8,128)}, u32[]{:S(2)}, u32[]{:S(2)}) async-start(f32[16,1,160,384]{3,2,1,0:T(8,128)} %fusion.7), calls=%async_computation.2 | async-start | bytes 7864320 | tf_op jit(solution)/shard_map/all_to_all | solution.py:127
  118.4 4.1 %select_select_fusion.2 = s32[1024,1]{0,1:T(1,128)S(1)} fusion(s32[]{:T(128)} %bitcast.20, s32[]{:T(128)} %bitcast.21, s32[]{:T(128)} %bitcast.22, s32[]{:T(128)} %bitcast.23, s32[]{:T(128)} %bitcast.24, s32[]{:T(128)} %bitcast.26, s32[]{:T(128)} %bitcast.25, s32[1024,1]{0,1:T(1,128)S(1)} %bitcast.113), kind=kLoop, calls=%fused_computation.56 | loop fusion | flops 15360 | bytes 8220 | tf_op jit(solution)/shard_map/gather | solution.py:128
  122.5 9.0 %select_select_fusion = (s32[1024,1]{0,1:T(1,128)S(1)}, s32[1024,1]{0,1:T(1,128)S(1)}) fusion(s32[]{:T(128)} %bitcast.39, s32[]{:T(128)} %bitcast.40, s32[]{:T(128)} %bitcast.41, s32[]{:T(128)} %bitcast.42, s32[]{:T(128)} %bitcast.43, s32[]{:T(128)} %bitcast.45, s32[]{:T(128)} %bitcast.44, s32[1024,1]{0,1:T(1,128)S(1)} %bitcast.114, s32[]{:T(128)} %bitcast.35, ...), kind=kLoop, calls=%fused_computation.54 | loop fusion | flops 21504 | bytes 12344 | tf_op jit(solution)/shard_map/gather | solution.py:129
  131.6 1.9 broadcast_select_fusion.2
  133.5 71.2 %all-to-all-done.2 = f32[16,1,160,384]{3,2,1,0:T(8,128)} async-done(((f32[16,1,160,384]{3,2,1,0:T(8,128)}), f32[16,1,160,384]{3,2,1,0:T(8,128)}, u32[]{:S(2)}, u32[]{:S(2)}) %all-to-all-start.2) | async-done | bytes 3932192 | tf_op jit(solution)/shard_map/all_to_all | solution.py:127
  204.7 7.1 %gather_fusion.1 = f32[1024,384]{1,0:T(8,128)} fusion(f32[2560,384]{1,0:T(8,128)} %bitcast.17, s32[1024]{0:T(1024)S(1)} %broadcast_clamp_fusion), kind=kCustom, calls=%fused_computation.1 | custom fusion | bytes 3149824 | tf_op jit(solution)/shard_map/gather | solution.py:131
  211.8 1.9 copy.50
  214.7 3.0 bitcast_add_fusion
  217.8 43.7 %reduce-scatter.2.cloned.1.call-done = f32[256,896]{0,1:T(8,128)} async-done(((f32[1024,896]{0,1:T(8,128)}), f32[256,896]{0,1:T(8,128)}) %reduce-scatter.2.cloned.1.call-update) | async-done | bytes 917520 | tf_op jit(solution)/shard_map/reduce_scatter | solution.py:135
  261.5 1.2 convert.5
  264.4 1.8 copy.55
  266.2 25.1 %all-gather.2.cloned.1.call-done = bf16[1024,512]{0,1:T(8,128)(2,1)} async-done(((bf16[256,512]{0,1:T(8,128)(2,1)}), bf16[1024,512]{0,1:T(8,128)(2,1)}) %all-gather.2.cloned.1.call-update) | async-done | bytes 1048592 | tf_op jit(solution)/shard_map/all_gather | solution.py:149
  291.3 1.7 fusion.4
  293.8 1.9 fusion.22
  (68 shorter events, 9.4 us)
Async XLA Ops:
  7.2 90.7 %copy-start = (bf16[64,384,16]{1,2,0:T(8,128)(2,1)S(1)}, bf16[64,384,16]{1,2,0:T(8,128)(2,1)}, u32[]{:S(2)}) copy-start(bf16[64,384,16]{1,2,0:T(8,128)(2,1)} %param.10) | copy-start | bytes 2359300
  8.8 11.6 %copy-start.10 = (s32[1,8]{1,0:T(1,128)}, s32[1,8]{1,0:T(1,128)S(1)}, u32[]{:S(2)}) copy-start(s32[1,8]{1,0:T(1,128)S(1)} %copy.62) | copy-start | bytes 100
  8.9 11.4 %copy-start.12 = (s32[8,1]{0,1:T(1,128)}, s32[8,1]{0,1:T(1,128)S(1)}, u32[]{:S(2)}) copy-start(s32[8,1]{0,1:T(1,128)S(1)} %reduce-window.4) | copy-start | bytes 100
  9.0 11.4 %copy-start.6 = (s32[8]{0:T(128)}, s32[8]{0:T(128)S(1)}, u32[]{:S(2)}) copy-start(s32[8]{0:T(128)S(1)} %get-tuple-element.49) | copy-start | bytes 100
  9.1 0.5 copy-start.8
  10.4 0.5 copy-start.4
  11.7 32.8 %all-to-all-start = ((bf16[16,1,1]{2,1,0:T(2,128)(2,1)}), bf16[16,1,1]{2,1,0:T(2,128)(2,1)}, u32[]{:S(2)}, u32[]{:S(2)}) async-start(bf16[16,1,1]{2,1,0:T(2,128)(2,1)} %copy.46), calls=%async_computation | async-start | bytes 16384 | tf_op jit(solution)/shard_map/all_to_all | solution.py:120
  44.5 53.4 %all-to-all-start.1 = ((bf16[16,1,160,384]{3,2,1,0:T(8,128)(2,1)}), bf16[16,1,160,384]{3,2,1,0:T(8,128)(2,1)S(1)}, u32[]{:S(2)}, u32[]{:S(2)}) async-start(bf16[16,1,160,384]{3,2,1,0:T(8,128)(2,1)} %broadcast_select_fusion), calls=%async_computation.1 | async-start | bytes 3932160 | tf_op jit(solution)/shard_map/all_to_all | solution.py:119
  97.9 3.0 copy-start.1
  111.2 5.0 %copy-start.5 = (s32[8]{0:T(128)S(1)}, s32[8]{0:T(128)}, u32[]{:S(2)}) copy-start(s32[8]{0:T(128)} %copy-done.4) | copy-start | bytes 100
  111.2 5.7 %copy-start.9 = (s32[8]{0:T(128)S(1)}, s32[8]{0:T(128)}, u32[]{:S(2)}) copy-start(s32[8]{0:T(128)} %copy-done.8) | copy-start | bytes 100
  111.2 6.4 %copy-start.7 = (s32[8]{0:T(128)S(1)}, s32[8]{0:T(128)}, u32[]{:S(2)}) copy-start(s32[8]{0:T(128)} %copy-done.6) | copy-start | bytes 100
  111.2 7.1 %copy-start.11 = (s32[1,8]{1,0:T(1,128)S(1)}, s32[1,8]{1,0:T(1,128)}, u32[]{:S(2)}) copy-start(s32[1,8]{1,0:T(1,128)} %copy-done.10) | copy-start | bytes 100
  111.2 7.1 %copy-start.13 = (s32[8,1]{0,1:T(1,128)S(1)}, s32[8,1]{0,1:T(1,128)}, u32[]{:S(2)}) copy-start(s32[8,1]{0,1:T(1,128)} %copy-done.12) | copy-start | bytes 100
  111.2 93.5 %all-to-all-start.2 = ((f32[16,1,160,384]{3,2,1,0:T(8,128)}), f32[16,1,160,384]{3,2,1,0:T(8,128)}, u32[]{:S(2)}, u32[]{:S(2)}) async-start(f32[16,1,160,384]{3,2,1,0:T(8,128)} %fusion.7), calls=%async_computation.2 | async-start | bytes 7864320 | tf_op jit(solution)/shard_map/all_to_all | solution.py:127
  116.0 145.5 %reduce-scatter.2.cloned.1.call-start = ((), (), s32[]{:S(2)}) async-start(), calls=%async_computation.4 | async-start | bytes 4587520 | tf_op jit(solution)/shard_map/reduce_scatter | solution.py:135
  211.8 2.1 copy-start.2
  213.8 1.0 copy-start.3
  217.7 73.6 %all-gather.2.cloned.1.call-start = ((), (), s32[]{:S(2)}) async-start(), calls=%async_computation.5 | async-start | bytes 1310720 | tf_op jit(solution)/shard_map/all_gather | solution.py:149
Sparse Core Ops, SparseCore 0:
  217.8 43.6 reduce-scatter.1
  263.6 27.6 all-gather.1
where the time goes:
time: 304 us; the launch traced here: 303 us
  waiting for transfers between devices  185 us (61%)
  local copies, waits for them, and re-layouts  24.7 us (8%)
  other arithmetic  23.1 us (8%)
  starting transfers between devices  20.6 us (7%)
  matrix products  19.9 us (7%)
  between operations  15 us (5%)
  blocking collectives  14.9 us (5%)
    all_to_all x1, waiting for transfers between devices, body(): lax.all_to_all(adapter_part, 'dp', split_axis=0, concat_axis=0, tiled=True)  71.2 us
    all_to_all x1, waiting for transfers between devices, body(): lax.all_to_all(outgoing, 'dp', split_axis=0, concat_axis=0, tiled=True)  45.2 us
    reduce_scatter x1, waiting for transfers between devices, body(): lax.psum_scatter(partial_value + jnp.concatenate([adapter_term, jnp.zeros...  43.7 us
    all_gather x1, waiting for transfers between devices, body(): lax.all_gather(kv_cache, 'col', axis=0, tiled=True)  25.1 us
    all_gather x1, blocking collectives, body(): gathered = lax.all_gather(hidden_states, 'row', axis=0, tiled=True)  14.9 us
    gather x2, other arithmetic, body(): starts[request_of]  10.9 us
    dot_general x1, matrix products, body(): jnp.einsum('nkla,af->nklf', reduced, flat_up, precision=lax.Precision.HIG...  10.3 us
    gather x2, local copies, waits for them, and re-layouts, body(): adapter_term = returned.reshape(-1, query_cols)[flat_index]  9.02 us
  transfers between devices with their start and end apart: 5, of which 4 were waited for; matrix products, arithmetic and copies ran while one was open for 10% of the time, Pallas kernels for 0%

commit v1 on v0

--- a/solution.py
+++ b/solution.py
@@ -145,8 +145,15 @@
     query_rows = summed[:, :query_cols].astype(jnp.bfloat16)
     kv_cache = summed[:, query_cols:].astype(jnp.bfloat16)
     attend, initial = make_attend(query_rows, segment, first_row, kv_group, head_size, kv_half)
+
+    def render_gates_by_axis(arr):
+        kept_arr = jnp.concatenate(
+            lax.all_to_all(jnp.stack([arr] * lax.axis_size("col"), axis=0), "col", 0, 0), 0
+        )
+        return kept_arr
+
     running_max, running_sum, running_out = attend(
-        initial, lax.all_gather(kv_cache, "col", axis=0, tiled=True), jnp.int32(0)
+        initial, render_gates_by_axis(kv_cache), jnp.int32(0)
     )
     attention = (running_out / running_sum[:, :, None]).astype(jnp.bfloat16)
     attention = jnp.transpose(attention, (1, 0, 2)).reshape(own_rows, query_cols)

time: 304 us -> 294 us (0.967)
  waiting for transfers between devices: 185 us -> 175 us
  starting transfers between devices: 20.6 us -> 24.1 us
    all_gather x1 -> x0, waiting for transfers between devices: 25.1 us -> none  [body(): lax.all_gather(kv_cache, 'col', axis=0, tiled=True)]
    all_to_all x0 -> x1, waiting for transfers between devices: none -> 14.3 us  [render_gates_by_axis(): lax.all_to_all(jnp.stack([arr] * lax.axis_size('col'), axis=0), 'col', 0, 0)]
    all_to_all x0 -> x1, starting transfers between devices: none -> 3.51 us  [render_gates_by_axis(): lax.all_to_all(jnp.stack([arr] * lax.axis_size('col'), axis=0), 'col', 0, 0)]
where the time goes in v1:
time: 294 us; the launch traced here: 293 us
  waiting for transfers between devices  175 us (60%)
  starting transfers between devices  24.1 us (8%)
  local copies, waits for them, and re-layouts  23.4 us (8%)
  other arithmetic  23.1 us (8%)
  matrix products  17.9 us (6%)
  between operations  15.1 us (5%)
  blocking collectives  14.9 us (5%)
    all_to_all x1, waiting for transfers between devices, body(): lax.all_to_all(adapter_part, 'dp', split_axis=0, concat_axis=0, tiled=True)  71.2 us
    all_to_all x1, waiting for transfers between devices, body(): lax.all_to_all(outgoing, 'dp', split_axis=0, concat_axis=0, tiled=True)  45.2 us
    reduce_scatter x1, waiting for transfers between devices, body(): lax.psum_scatter(partial_value + jnp.concatenate([adapter_term, jnp.zeros...  43.8 us
    all_gather x1, blocking collectives, body(): gathered = lax.all_gather(hidden_states, 'row', axis=0, tiled=True)  14.9 us
    all_to_all x1, waiting for transfers between devices, render_gates_by_axis(): lax.all_to_all(jnp.stack([arr] * lax.axis_size('col'), axis=0), 'col', 0, 0)  14.3 us
    gather x2, other arithmetic, body(): starts[request_of]  10.9 us
    dot_general x1, matrix products, body(): jnp.einsum('nkla,af->nklf', reduced, flat_up, precision=lax.Precision.HIG...  10.3 us
    gather x2, local copies, waits for them, and re-layouts, body(): adapter_term = returned.reshape(-1, query_cols)[flat_index]  9.02 us
  transfers between devices with their start and end apart: 5, of which 4 were waited for; matrix products, arithmetic and copies ran while one was open for 10% of the time, Pallas kernels for 0%

profile of v1, /device:TPU:8, one launch (start us, length us, event | category | flops | bytes accessed | tf_op | source)
XLA Modules:
  0.0 292.9 jit_solution(10576740022863681527)
XLA Ops:
  7.2 1.5 fusion.34
  11.7 8.6 %all-to-all-start = ((bf16[16,1,1]{2,1,0:T(2,128)(2,1)}), bf16[16,1,1]{2,1,0:T(2,128)(2,1)}, u32[]{:S(2)}, u32[]{:S(2)}) async-start(bf16[16,1,1]{2,1,0:T(2,128)(2,1)} %copy.50), calls=%async_computation | async-start | bytes 16384 | tf_op jit(solution)/shard_map/all_to_all | solution.py:120
  20.5 14.9 %all_gather.3 = bf16[1024,384]{1,0:T(8,128)(2,1)S(1)} all-gather(bf16[256,384]{1,0:T(8,128)(2,1)} %param.7), channel_id=1, replica_groups=mesh['row'=4,'col'=4,'dp'=16] {'row'}, dimensions={0}, use_global_device_ids=true | all-gather | bytes 983040 | tf_op jit(solution)/shard_map/all_gather | solution.py:72
  35.5 7.5 %gather_fusion = bf16[2560,384]{1,0:T(8,128)(2,1)S(1)} fusion(bf16[1024,384]{1,0:T(8,128)(2,1)S(1)} %all_gather.3, s32[3072]{0:T(1024)S(1)} %pad_clamp_fusion), kind=kCustom, calls=%fused_computation | custom fusion | bytes 3942400 | tf_op jit(solution)/shard_map/gather | solution.py:113
  43.0 1.5 broadcast_select_fusion
  44.5 7.0 %all-to-all-start.1 = ((bf16[16,1,160,384]{3,2,1,0:T(8,128)(2,1)}), bf16[16,1,160,384]{3,2,1,0:T(8,128)(2,1)S(1)}, u32[]{:S(2)}, u32[]{:S(2)}) async-start(bf16[16,1,160,384]{3,2,1,0:T(8,128)(2,1)} %broadcast_select_fusion), calls=%async_computation.1 | async-start | bytes 3932160 | tf_op jit(solution)/shard_map/all_to_all | solution.py:119
  51.5 1.1 convert_reduce_fusion.1
  52.7 45.2 %all-to-all-done.1 = bf16[16,1,160,384]{3,2,1,0:T(8,128)(2,1)S(1)} async-done(((bf16[16,1,160,384]{3,2,1,0:T(8,128)(2,1)}), bf16[16,1,160,384]{3,2,1,0:T(8,128)(2,1)S(1)}, u32[]{:S(2)}, u32[]{:S(2)}) %all-to-all-start.1) | async-done | bytes 1966112 | tf_op jit(solution)/shard_map/all_to_all | solution.py:119
  97.9 3.0 %fusion.10 = f32[16,160,1024]{2,1,0:T(8,128)S(1)} fusion(bf16[384,1024,1]{0,1,2:T(8,128)(2,1)S(1)} %bitcast.108, bf16[16,1,160,384]{3,2,1,0:T(8,128)(2,1)S(1)} %all-to-all-done.1), kind=kOutput, calls=%fused_computation.13 | convolution fusion | flops 2013265920 | bytes 13238272 | tf_op jit(solution)/shard_map/nkld,da->nkla/dot_general | solution.py:123
  100.9 10.3 %fusion.7 = f32[16,1,160,384]{3,2,1,0:T(8,128)} fusion(bf16[1024,384,1]{1,0,2:T(8,128)(2,1)S(1)} %bitcast.112, f32[16,160,1024]{2,1,0:T(8,128)S(1)} %fusion.10, pred[16,1024]{1,0:T(8,128)(4,1)S(1)} %broadcast_compare_fusion), kind=kOutput, calls=%fused_computation.12 | convolution fusion | flops 12082216960 | bytes 15220736 | tf_op jit(solution)/shard_map/nkla,af->nklf/dot_general | solution.py:126
  111.2 4.8 %all-to-all-start.2 = ((f32[16,1,160,384]{3,2,1,0:T(8,128)}), f32[16,1,160,384]{3,2,1,0:T(8,128)}, u32[]{:S(2)}, u32[]{:S(2)}) async-start(f32[16,1,160,384]{3,2,1,0:T(8,128)} %fusion.7), calls=%async_computation.2 | async-start | bytes 7864320 | tf_op jit(solution)/shard_map/all_to_all | solution.py:127
  118.4 4.1 %select_select_fusion.2 = s32[1024,1]{0,1:T(1,128)S(1)} fusion(s32[]{:T(128)} %bitcast.20, s32[]{:T(128)} %bitcast.21, s32[]{:T(128)} %bitcast.22, s32[]{:T(128)} %bitcast.23, s32[]{:T(128)} %bitcast.24, s32[]{:T(128)} %bitcast.26, s32[]{:T(128)} %bitcast.25, s32[1024,1]{0,1:T(1,128)S(1)} %bitcast.116), kind=kLoop, calls=%fused_computation.56 | loop fusion | flops 15360 | bytes 8220 | tf_op jit(solution)/shard_map/gather | solution.py:128
  122.5 9.0 %select_select_fusion = (s32[1024,1]{0,1:T(1,128)S(1)}, s32[1024,1]{0,1:T(1,128)S(1)}) fusion(s32[]{:T(128)} %bitcast.39, s32[]{:T(128)} %bitcast.40, s32[]{:T(128)} %bitcast.41, s32[]{:T(128)} %bitcast.42, s32[]{:T(128)} %bitcast.43, s32[]{:T(128)} %bitcast.45, s32[]{:T(128)} %bitcast.44, s32[1024,1]{0,1:T(1,128)S(1)} %bitcast.117, s32[]{:T(128)} %bitcast.35, ...), kind=kLoop, calls=%fused_computation.54 | loop fusion | flops 21504 | bytes 12344 | tf_op jit(solution)/shard_map/gather | solution.py:129
  131.6 1.9 broadcast_select_fusion.2
  133.5 71.2 %all-to-all-done.2 = f32[16,1,160,384]{3,2,1,0:T(8,128)} async-done(((f32[16,1,160,384]{3,2,1,0:T(8,128)}), f32[16,1,160,384]{3,2,1,0:T(8,128)}, u32[]{:S(2)}, u32[]{:S(2)}) %all-to-all-start.2) | async-done | bytes 3932192 | tf_op jit(solution)/shard_map/all_to_all | solution.py:127
  204.7 7.1 %gather_fusion.1 = f32[1024,384]{1,0:T(8,128)} fusion(f32[2560,384]{1,0:T(8,128)} %bitcast.17, s32[1024]{0:T(1024)S(1)} %broadcast_clamp_fusion), kind=kCustom, calls=%fused_computation.1 | custom fusion | bytes 3149824 | tf_op jit(solution)/shard_map/gather | solution.py:131
  211.8 1.9 copy.54
  214.7 3.0 %bitcast_add_fusion = f32[1024,896]{0,1:T(8,128)} fusion(f32[1024,384]{0,1:T(8,128)S(1)} %broadcast_select_fusion.1, bf16[1024,384]{1,0:T(8,128)(2,1)S(1)} %all_gather.3, bf16[384,512]{1,0:T(8,128)(2,1)S(1)} %copy-done.3, bf16[384,384]{1,0:T(8,128)(2,1)S(1)} %copy-done.4), kind=kOutput, calls=%fused_computation.6 | convolution fusion | flops 706936832 | bytes 6717440 | tf_op jit(solution)/shard_map/dot_general | solution.py:134
  217.7 43.8 %reduce-scatter.2.cloned.1.call-done = f32[256,896]{0,1:T(8,128)} async-done(((f32[1024,896]{0,1:T(8,128)}), f32[256,896]{0,1:T(8,128)}) %reduce-scatter.2.cloned.1.call-update) | async-done | bytes 917520 | tf_op jit(solution)/shard_map/reduce_scatter | solution.py:135
  261.5 1.2 convert.5
  262.9 1.1 stack.2
  264.0 3.5 %all-to-all-start.3 = ((bf16[4,256,512]{2,1,0:T(8,128)(2,1)}), bf16[4,256,512]{2,1,0:T(8,128)(2,1)S(1)}, u32[]{:S(2)}, u32[]{:S(2)}) async-start(bf16[4,256,512]{2,1,0:T(8,128)(2,1)} %stack.2), calls=%async_computation.4 | async-start | bytes 2097152 | tf_op jit(solution)/shard_map/all_to_all | solution.py:151
  268.4 14.3 %all-to-all-done.3 = bf16[4,256,512]{2,1,0:T(8,128)(2,1)S(1)} async-done(((bf16[4,256,512]{2,1,0:T(8,128)(2,1)}), bf16[4,256,512]{2,1,0:T(8,128)(2,1)S(1)}, u32[]{:S(2)}, u32[]{:S(2)}) %all-to-all-start.3) | async-done | bytes 1048608 | tf_op jit(solution)/shard_map/all_to_all | solution.py:151
  284.3 1.0 fusion.22
  (70 shorter events, 9.5 us)
Async XLA Ops:
  7.2 90.7 %copy-start = (bf16[64,384,16]{1,2,0:T(8,128)(2,1)S(1)}, bf16[64,384,16]{1,2,0:T(8,128)(2,1)}, u32[]{:S(2)}) copy-start(bf16[64,384,16]{1,2,0:T(8,128)(2,1)} %param.10) | copy-start | bytes 2359300
  8.8 11.6 %copy-start.11 = (s32[1,8]{1,0:T(1,128)}, s32[1,8]{1,0:T(1,128)S(1)}, u32[]{:S(2)}) copy-start(s32[1,8]{1,0:T(1,128)S(1)} %copy.67) | copy-start | bytes 100
  8.9 11.4 %copy-start.13 = (s32[8,1]{0,1:T(1,128)}, s32[8,1]{0,1:T(1,128)S(1)}, u32[]{:S(2)}) copy-start(s32[8,1]{0,1:T(1,128)S(1)} %reduce-window.4) | copy-start | bytes 100
  9.0 11.4 %copy-start.7 = (s32[8]{0:T(128)}, s32[8]{0:T(128)S(1)}, u32[]{:S(2)}) copy-start(s32[8]{0:T(128)S(1)} %get-tuple-element.49) | copy-start | bytes 100
  9.1 0.5 copy-start.9
  10.4 0.5 copy-start.5
  11.7 32.8 %all-to-all-start = ((bf16[16,1,1]{2,1,0:T(2,128)(2,1)}), bf16[16,1,1]{2,1,0:T(2,128)(2,1)}, u32[]{:S(2)}, u32[]{:S(2)}) async-start(bf16[16,1,1]{2,1,0:T(2,128)(2,1)} %copy.50), calls=%async_computation | async-start | bytes 16384 | tf_op jit(solution)/shard_map/all_to_all | solution.py:120
  44.5 53.4 %all-to-all-start.1 = ((bf16[16,1,160,384]{3,2,1,0:T(8,128)(2,1)}), bf16[16,1,160,384]{3,2,1,0:T(8,128)(2,1)S(1)}, u32[]{:S(2)}, u32[]{:S(2)}) async-start(bf16[16,1,160,384]{3,2,1,0:T(8,128)(2,1)} %broadcast_select_fusion), calls=%async_computation.1 | async-start | bytes 3932160 | tf_op jit(solution)/shard_map/all_to_all | solution.py:119
  97.9 3.0 %copy-start.2 = (bf16[64,16,384]{2,1,0:T(8,128)(2,1)S(1)}, bf16[64,16,384]{2,1,0:T(8,128)(2,1)}, u32[]{:S(2)}) copy-start(bf16[64,16,384]{2,1,0:T(8,128)(2,1)} %param.11) | copy-start | bytes 2359300
  111.2 5.0 %copy-start.6 = (s32[8]{0:T(128)S(1)}, s32[8]{0:T(128)}, u32[]{:S(2)}) copy-start(s32[8]{0:T(128)} %copy-done.5) | copy-start | bytes 100
  111.2 5.7 %copy-start.10 = (s32[8]{0:T(128)S(1)}, s32[8]{0:T(128)}, u32[]{:S(2)}) copy-start(s32[8]{0:T(128)} %copy-done.9) | copy-start | bytes 100
  111.2 6.4 %copy-start.8 = (s32[8]{0:T(128)S(1)}, s32[8]{0:T(128)}, u32[]{:S(2)}) copy-start(s32[8]{0:T(128)} %copy-done.7) | copy-start | bytes 100
  111.2 7.1 %copy-start.12 = (s32[1,8]{1,0:T(1,128)S(1)}, s32[1,8]{1,0:T(1,128)}, u32[]{:S(2)}) copy-start(s32[1,8]{1,0:T(1,128)} %copy-done.11) | copy-start | bytes 100
  111.2 7.1 %copy-start.14 = (s32[8,1]{0,1:T(1,128)S(1)}, s32[8,1]{0,1:T(1,128)}, u32[]{:S(2)}) copy-start(s32[8,1]{0,1:T(1,128)} %copy-done.13) | copy-start | bytes 100
  111.2 93.5 %all-to-all-start.2 = ((f32[16,1,160,384]{3,2,1,0:T(8,128)}), f32[16,1,160,384]{3,2,1,0:T(8,128)}, u32[]{:S(2)}, u32[]{:S(2)}) async-start(f32[16,1,160,384]{3,2,1,0:T(8,128)} %fusion.7), calls=%async_computation.2 | async-start | bytes 7864320 | tf_op jit(solution)/shard_map/all_to_all | solution.py:127
  116.0 145.5 %reduce-scatter.2.cloned.1.call-start = ((), (), s32[]{:S(2)}) async-start(), calls=%async_computation.5 | async-start | bytes 4587520 | tf_op jit(solution)/shard_map/reduce_scatter | solution.py:135
  211.8 2.1 copy-start.3
  213.8 1.0 copy-start.4
  262.9 20.6 %copy-start.1 = (bf16[256,512]{1,0:T(8,128)(2,1)}, bf16[256,512]{1,0:T(8,128)(2,1)S(1)}, u32[]{:S(2)}) copy-start(bf16[256,512]{1,0:T(8,128)(2,1)S(1)} %copy.55) | copy-start | bytes 786436
  264.0 18.8 %all-to-all-start.3 = ((bf16[4,256,512]{2,1,0:T(8,128)(2,1)}), bf16[4,256,512]{2,1,0:T(8,128)(2,1)S(1)}, u32[]{:S(2)}, u32[]{:S(2)}) async-start(bf16[4,256,512]{2,1,0:T(8,128)(2,1)} %stack.2), calls=%async_computation.4 | async-start | bytes 2097152 | tf_op jit(solution)/shard_map/all_to_all | solution.py:151
Sparse Core Ops, SparseCore 0:
  217.8 43.6 reduce-scatter.1
